TPU v7x, 512 devices: a whole 4x4x16 slice. The times are simulated.
512 devices in a mesh: seq: 64 (over x, z), tp: 8 (over y, core).
Axes of the slice: x: 4, y: 4, z: 16, core: 2. Of those that a mesh axis runs over, the one named last changes fastest.
Arguments:
- hidden_in: bfloat16 [8192, 2048], P('seq', 'tp'), may hold values from -3 to 3
- norm_gain: float32 [2048], replicated, may hold values from 0.1 to 1.9
- w_query: bfloat16 [2048, 2048], P(None, 'tp'), may hold values from -0.125 to 0.125
- w_key: bfloat16 [2048, 1024], P(None, 'tp'), may hold values from -0.125 to 0.125
- w_value: bfloat16 [2048, 1024], P(None, 'tp'), may hold values from -0.125 to 0.125
- w_headgate: bfloat16 [2048, 16], P(None, 'tp'), may hold values from -0.125 to 0.125
- w_out: bfloat16 [2048, 2048], P('tp'), may hold values from -0.125 to 0.125
- q_gain: float32 [128], replicated, may hold values from 1.5 to 4
- k_gain: float32 [128], replicated, may hold values from 0.1 to 1.9
- cache_keys: bfloat16 [2, 8192, 1024], P(None, 'seq', 'tp'), as said below
- cache_values: bfloat16 [2, 8192, 1024], P(None, 'seq', 'tp'), may hold values from -6 to 6
- cached_len: int32 [8], replicated, may hold values from 0 to 8192, as said below
- group_of: int32 [8], replicated, may hold values from 0 to 1, as said below
Outputs:
- layer_out: bfloat16 [8192, 2048], P('seq', 'tp')
Inputs may be any that keep to these rules, and one draw needn't show every extreme that they name: `cache_keys`: keys of the cached positions, of order one and larger. `cached_len`: some request attends to all 8192 cached positions of its prompt, and some to none. `group_of`: every shared prompt is used by some request.
All inputs are finite; a program needn't handle non-finite values.
Results may differ from a plain program's by a relative error of at most 0.018.
Values may be sent and summed in bfloat16 or wider, within the bound.
No kernel may reach another device: no remote copies, remote signals or barrier semaphores. Data moves between devices by JAX's collectives and lax.ppermute only.
A program may use at most 64 MiB of HBM per device.

v0:
```python
import math
import jax
import jax.numpy as jnp
from jax import lax
from jax.sharding import Mesh, PartitionSpec as P

SPAN = 1024
norm_eps = 1e-06
rope_base = 1000000.0
masked_score = -1e30


def shifted(value, axis, by):
    peers = lax.axis_size(axis)
    pairs = [(i, i + by) for i in range(peers) if 0 <= i + by < peers]
    return lax.ppermute(value, axis, pairs)


def head_norm(vec, gain):
    return vec * lax.rsqrt(jnp.mean(vec * vec, -1, keepdims=True) + norm_eps) * gain


def rotate(vec, positions):
    half = vec.shape[-1] // 2
    freq = jnp.exp(
        jnp.arange(half, dtype=jnp.float32) * (-2.0 * math.log(rope_base) / vec.shape[-1])
    )
    angle = positions.astype(jnp.float32)[:, None] * freq[None, :]
    shape_out = (vec.shape[0],) + (1,) * (vec.ndim - 2) + (half,)
    cosine = jnp.cos(angle).reshape(shape_out)
    sine = jnp.sin(angle).reshape(shape_out)
    first = vec[..., :half]
    second = vec[..., half:]
    return jnp.concatenate([first * cosine - second * sine, second * cosine + first * sine], -1)


def attend(state_now, queries, keys_block, values_block, visible):
    running_max, running_sum, running_acc = state_now
    scores = jnp.einsum(
        "tcgd,kcd->tcgk", queries, keys_block, preferred_element_type=jnp.float32
    ) * queries.shape[-1] ** (-0.5)
    scores = jnp.where(visible[:, None, None, :], scores, masked_score)
    new_max = jnp.maximum(running_max, jnp.max(scores, -1))
    rescale = jnp.exp(running_max - new_max)
    expo = jnp.exp(scores - new_max[..., None])
    new_sum = running_sum * rescale + jnp.sum(expo, -1)
    update = jnp.einsum(
        "tcgk,kcd->tcgd",
        expo.astype(jnp.bfloat16),
        values_block,
        preferred_element_type=jnp.float32,
    )
    return (new_max, new_sum, running_acc * rescale[..., None] + update)


def per_device(
    hidden_in,
    norm_gain,
    w_query,
    w_key,
    w_value,
    w_headgate,
    w_out,
    q_gain,
    k_gain,
    cache_keys,
    cache_values,
    cached_len,
    group_of,
):
    tok_rows = hidden_in.shape[0]
    head_dim = q_gain.shape[0]
    kv_local = w_key.shape[1] // head_dim
    heads_local = w_query.shape[1] // head_dim
    group_size = heads_local // kv_local
    per_request = SPAN // tok_rows
    ring_x = lax.axis_size("sx")
    ring_z = lax.axis_size("sz")
    req_count = ring_x * ring_z // per_request
    pair = ring_z // req_count
    x_index = lax.axis_index("sx")
    z_index = lax.axis_index("sz")
    seq_index = x_index * ring_z + z_index
    request = seq_index % req_count
    local_part = seq_index // req_count
    parity = z_index // req_count
    length = cached_len[request]
    peer_groups = group_of[jnp.arange(ring_z, dtype=jnp.int32) % req_count]
    cache_both = jnp.stack([cache_keys, cache_values], 1)
    incoming = lax.all_to_all(cache_both[peer_groups], "sz", 0, 0, tiled=True)
    cache_rows = ring_z * cache_keys.shape[1]
    keys_cache = incoming[:, 0].reshape(cache_rows, kv_local, head_dim)
    values_cache = incoming[:, 1].reshape(cache_rows, kv_local, head_dim)
    cache_pos = x_index * cache_rows + jnp.arange(cache_rows, dtype=jnp.int32)
    gathered = lax.all_gather(hidden_in, "tp", axis=1, tiled=True)
    widened = gathered.astype(jnp.float32)
    normed = (
        widened * lax.rsqrt(jnp.mean(widened * widened, -1, keepdims=True) + norm_eps) * norm_gain
    ).astype(jnp.bfloat16)
    positions = length + local_part * tok_rows + jnp.arange(tok_rows, dtype=jnp.int32)
    query_raw = jnp.dot(normed, w_query, preferred_element_type=jnp.float32).reshape(
        tok_rows, kv_local, group_size, head_dim
    )
    queries = rotate(head_norm(query_raw, q_gain), positions).astype(jnp.bfloat16)
    key_raw = jnp.dot(normed, w_key, preferred_element_type=jnp.float32).reshape(
        tok_rows, kv_local, head_dim
    )
    keys_new = rotate(head_norm(key_raw, k_gain), positions).astype(jnp.bfloat16)
    values_new = (
        jnp.dot(normed, w_value, preferred_element_type=jnp.float32)
        .astype(jnp.bfloat16)
        .reshape(tok_rows, kv_local, head_dim)
    )
    gates = jax.nn.sigmoid(jnp.dot(normed, w_headgate, preferred_element_type=jnp.float32)).reshape(
        tok_rows, kv_local, group_size
    )
    partner_pairs = [(z, (z + req_count) % ring_z) for z in range(ring_z)]
    partner_keys, partner_values = lax.ppermute((keys_new, values_new), "sz", partner_pairs)
    partner_part = x_index * pair + (pair - 1 - parity)
    all_queries = lax.all_gather(queries, "sx", axis=0, tiled=True)
    query_tok = (
        (jnp.arange(ring_x, dtype=jnp.int32) * pair + parity)[:, None] * tok_rows
        + jnp.arange(tok_rows, dtype=jnp.int32)[None, :]
    ).reshape(-1)
    row_ids = jnp.arange(tok_rows, dtype=jnp.int32)
    key_tok = jnp.concatenate([local_part * tok_rows + row_ids, partner_part * tok_rows + row_ids])
    keys_all = jnp.concatenate([keys_cache, keys_new, partner_keys], 0)
    values_all = jnp.concatenate([values_cache, values_new, partner_values], 0)
    query_count = query_tok.shape[0]
    visible = jnp.concatenate(
        [
            jnp.broadcast_to((cache_pos < length)[None, :], (query_count, cache_rows)),
            key_tok[None, :] <= query_tok[:, None],
        ],
        1,
    )
    scores = jnp.einsum(
        "tcgd,kcd->tcgk", all_queries, keys_all, preferred_element_type=jnp.float32
    ) * head_dim ** (-0.5)
    seen = visible[:, None, None, :]
    scores = jnp.where(seen, scores, masked_score)
    top = jnp.max(scores, -1)
    expo = jnp.where(seen, jnp.exp(scores - top[..., None]), 0.0)
    total = jnp.sum(expo, -1)
    acc = jnp.einsum(
        "tcgk,kcd->tcgd", expo.astype(jnp.bfloat16), values_all, preferred_element_type=jnp.float32
    )
    stats = jnp.stack([top, total], -1).reshape(ring_x, tok_rows, kv_local, group_size, 2)
    acc = acc.reshape(ring_x, tok_rows, kv_local, group_size, head_dim)
    stats_in = lax.all_to_all(stats, "sx", 0, 0, tiled=True)
    acc_in = lax.all_to_all(acc, "sx", 0, 0, tiled=True)
    best = jnp.max(stats_in[..., 0], 0)
    factor = jnp.exp(stats_in[..., 0] - best[None])
    total = jnp.sum(stats_in[..., 1] * factor, 0)
    summed_acc = jnp.sum(acc_in * factor[..., None], 0)
    mixed = (
        (summed_acc / total[..., None] * gates[..., None])
        .astype(jnp.bfloat16)
        .reshape(tok_rows, heads_local * head_dim)
    )
    partial_out = jnp.dot(mixed, w_out, preferred_element_type=jnp.float32)
    tp_size = lax.axis_size("tp")
    pieces = partial_out.astype(jnp.bfloat16).reshape(tok_rows, tp_size, -1)
    arrived = lax.all_to_all(pieces, "tp", 1, 1, tiled=True)
    summed = jnp.sum(arrived.astype(jnp.float32), 1)
    return (hidden_in.astype(jnp.float32) + summed).astype(jnp.bfloat16)


def solution(mesh):
    seq_size = mesh.shape["seq"]
    tp_size = mesh.shape["tp"]
    req_count = seq_size // (SPAN // 128)
    ring_z = 2 * req_count
    ring_x = seq_size // ring_z
    split_mesh = Mesh(mesh.devices.reshape(ring_x, ring_z, tp_size), ("sx", "sz", "tp"))
    seq = ("sx", "sz")
    in_specs = (
        P(seq, "tp"),
        P(),
        P(None, "tp"),
        P(None, "tp"),
        P(None, "tp"),
        P(None, "tp"),
        P("tp", None),
        P(),
        P(),
        P(None, seq, "tp"),
        P(None, seq, "tp"),
        P(),
        P(),
    )
    out_specs = P(seq, "tp")
    return jax.shard_map(
        per_device, mesh=split_mesh, in_specs=in_specs, out_specs=out_specs, check_vma=False
    )
```

profile of v0, /device:TPU:32, one launch (start us, length us, event | category | flops | bytes accessed | tf_op | source)
XLA Modules:
  0.0 155.3 jit_solution(10557558886728345072)
XLA Ops:
  0.0 14.0 %all_gather.6 = bf16[128,2048]{1,0:T(8,128)(2,1)S(1)} all-gather(bf16[128,256]{1,0:T(8,128)(2,1)} %param.13), channel_id=1, replica_groups=mesh['sx'=4,'sz'=16,'tp'=8] {'tp'}, dimensions={1}, use_global_device_ids=true | all-gather | bytes 589824 | tf_op jit(solution)/shard_map/all_gather | solution.py:95
  14.2 2.0 %fusion.10 = bf16[128,1,128]{2,0,1:T(8,128)(2,1)} fusion(bf16[2048,128]{1,0:T(8,128)(2,1)} %param.17, bf16[128,2048]{1,0:T(8,128)(2,1)S(1)} %all_gather.6, f32[2048]{0:T(1024)} %param.14, f32[128]{0:T(128)S(1)} %add_rsqrt_fusion.2), kind=kOutput, calls=%fused_computation.16 | convolution fusion | flops 68173824 | bytes 1090048 | tf_op jit(solution)/shard_map/dot_general | solution.py:110
  16.2 14.8 %collective-permute-start = (bf16[128,1,128]{2,0,1:T(8,128)(2,1)}, bf16[128,1,128]{2,0,1:T(8,128)(2,1)}, u32[]{:S(2)}, u32[]{:S(2)}) collective-permute-start(bf16[128,1,128]{2,0,1:T(8,128)(2,1)} %fusion.10), channel_id=1, source_target_pairs={{0,64},{8,72},{16,80},{24,88},{32,96},{40,104},{48,112},{56,120},{... | collective-permute-start | bytes 98312 | tf_op jit(solution)/shard_map/ppermute | solution.py:118
  31.1 1.3 gather_fusion
  33.3 1.7 %gather_fusion.1 = bf16[16,2,128,128]{3,2,1,0:T(8,128)(2,1)} fusion(bf16[2,2,128,128]{3,2,0,1:T(8,128)(2,1)S(1)} %pad_maximum_fusion, s32[1024]{0:T(1024)S(1)} %pad_clamp_fusion), kind=kCustom, calls=%fused_computation.1 | custom fusion | bytes 2097216 | tf_op jit(solution)/shard_map/gather | solution.py:90
  35.0 6.0 %all-to-all-start = ((bf16[16,2,128,128]{3,2,1,0:T(8,128)(2,1)}), bf16[16,2,128,128]{3,2,1,0:T(8,128)(2,1)S(1)}, u32[]{:S(2)}, u32[]{:S(2)}) async-start(bf16[16,2,128,128]{3,2,1,0:T(8,128)(2,1)} %gather_fusion.1), calls=%async_computation | async-start | bytes 2097152 | tf_op jit(solution)/shard_map/all_to_all | solution.py:90
  42.8 1.5 multiply_reduce_fusion.2
  45.9 11.2 %collective-permute-start.1 = (bf16[128,1,128]{0,2,1:T(8,128)(2,1)}, bf16[128,1,128]{0,2,1:T(8,128)(2,1)}, u32[]{:S(2)}, u32[]{:S(2)}) collective-permute-start(bf16[128,1,128]{0,2,1:T(8,128)(2,1)} %pad_maximum_fusion.2), channel_id=1, source_target_pairs={{0,64},{8,72},{16,80},{24,88},{32,96},{40,104},{48,112},{56,120},{... | collective-permute-start | bytes 98312 | tf_op jit(solution)/shard_map/ppermute | solution.py:118
  57.1 1.6 %fusion.49 = f32[128,256]{1,0:T(8,128)S(1)} fusion(bf16[2048,256]{1,0:T(8,128)(2,1)} %param.15, bf16[128,2048]{1,0:T(8,128)(2,1)S(1)} %all_gather.6, f32[2048]{0:T(1024)} %param.14, f32[128]{0:T(128)S(1)} %add_rsqrt_fusion.2), kind=kOutput, calls=%fused_computation.98 | convolution fusion | flops 135266304 | bytes 1712640 | tf_op jit(solution)/shard_map/dot_general | solution.py:101
  60.9 2.2 %pad_add_fusion = pred[512,2304]{0,1:T(8,128)(4,1)S(1)} fusion(pred[512,256]{0,1:T(8,128)(4,1)S(1)} %broadcast_compare_fusion, pred[2304]{0:T(1024)(128)(4,1)S(1)} %pad.9.clone), kind=kLoop, calls=%fused_computation.9 | loop fusion | flops 1179648 | bytes 1313024 | tf_op jit(solution)/shard_map/concatenate | solution.py:130
  63.1 12.6 %all_gather.7 = bf16[512,1,2,128]{3,0,2,1:T(8,128)(2,1)S(1)} all-gather(bf16[128,1,2,128]{3,0,2,1:T(8,128)(2,1)S(1)} %pad_maximum_fusion.1), channel_id=1, replica_groups=mesh['sx'=4,'sz'=16,'tp'=8] {'sx'}, dimensions={0}, use_global_device_ids=true | all-gather | bytes 327680 | tf_op jit(solution)/shard_map/all_gather | solution.py:120
  75.8 1.5 copy.58
  77.2 1.5 copy.60
  78.7 1.5 copy.59
  80.1 18.6 %collective-permute-done.1 = bf16[128,1,128]{0,2,1:T(8,128)(2,1)} collective-permute-done((bf16[128,1,128]{0,2,1:T(8,128)(2,1)}, bf16[128,1,128]{0,2,1:T(8,128)(2,1)}, u32[]{:S(2)}, u32[]{:S(2)}) %collective-permute-start.1) | collective-permute-done | bytes 32800 | tf_op jit(solution)/shard_map/ppermute | solution.py:118
  98.7 1.5 copy.61
  101.2 1.2 copy.72
  102.5 6.7 %fusion = (f32[512,2]{0,1:T(2,128)S(1)}, f32[2304,512,2]{1,0,2:T(8,128)}) fusion(pred[512,2304]{0,1:T(8,128)(4,1)S(1)} %pad_add_fusion, bf16[512,1,2,128]{3,0,2,1:T(8,128)(2,1)S(1)} %all_gather.7, bf16[128,1,128]{2,0,1:T(8,128)(2,1)} %copy.61, bf16[128,1,128]{2,0,1:T(8,128)(2,1)} %copy.60, bf16[2048,1,128]{2,0,1:T(8,128)(2,1)} %bitcast.102), kind=kOutput, calls=%fused_computation.4 | convolution fusion | flops 612826112 | bytes 11472896 | tf_op jit(solution)/shard_map/tcgd,kcd->tcgk/dot_general | solution.py:137
  109.3 6.1 %fusion.1 = f32[512,2]{0,1:T(2,128)S(1)} fusion(f32[2304,512,2]{1,0,2:T(8,128)} %get-tuple-element.16, f32[512,2]{0,1:T(2,128)S(1)} %get-tuple-element.15, pred[512,2304]{0,1:T(8,128)(4,1)S(1)} %pad_add_fusion), kind=kLoop, calls=%fused_computation.5 | loop fusion | flops 11795456 | bytes 10625024 | tf_op jit(solution)/shard_map/reduce_sum | solution.py:144
  116.0 4.3 %all-to-all-start.2 = ((f32[4,128,1,2,2]{1,3,4,2,0:T(2,128)}), f32[4,128,1,2,2]{1,3,4,2,0:T(2,128)S(1)}, u32[]{:S(2)}, u32[]{:S(2)}) async-start(f32[4,128,1,2,2]{1,3,4,2,0:T(2,128)} %copy.66), calls=%async_computation.2 | async-start | bytes 16384 | tf_op jit(solution)/shard_map/all_to_all | solution.py:150
  120.3 5.1 %fusion.7 = f32[1,2,16,4,8,128]{5,4,3,2,1,0:T(8,128)S(1)} fusion(f32[2304,512,2]{1,0,2:T(8,128)} %get-tuple-element.16, f32[512,2]{0,1:T(2,128)S(1)} %get-tuple-element.15, pred[512,2304]{0,1:T(8,128)(4,1)S(1)} %pad_add_fusion, bf16[128,1,128]{0,2,1:T(8,128)(2,1)S(1)} %copy-done.3, bf16[128,1,128]{0,2,1:T(8,128)(2,1)S(1)} %copy-done.2, ...), kind=kOutput, calls=%fused_computation.14 | convolution fusion | flops 617545728 | bytes 11735040 | tf_op jit(solution)/shard_map/tcgk,kcd->tcgd/dot_general | solution.py:145
  126.2 4.8 %all-to-all-start.1 = ((f32[4,128,1,2,128]{1,4,3,2,0:T(8,128)}), f32[4,128,1,2,128]{1,4,3,2,0:T(8,128)S(1)}, u32[]{:S(2)}, u32[]{:S(2)}) async-start(f32[4,128,1,2,128]{1,4,3,2,0:T(8,128)} %bitcast.98), calls=%async_computation.1 | async-start | bytes 1048576 | tf_op jit(solution)/shard_map/all_to_all | solution.py:151
  131.1 9.0 %all-to-all-done.1 = f32[4,128,1,2,128]{1,4,3,2,0:T(8,128)S(1)} async-done(((f32[4,128,1,2,128]{1,4,3,2,0:T(8,128)}), f32[4,128,1,2,128]{1,4,3,2,0:T(8,128)S(1)}, u32[]{:S(2)}, u32[]{:S(2)}) %all-to-all-start.1) | async-done | bytes 524320 | tf_op jit(solution)/shard_map/all_to_all | solution.py:151
  140.6 14.0 %all_to_all.20 = bf16[128,8,256]{2,0,1:T(8,128)(2,1)S(1)} all-to-all(bf16[128,8,256]{2,0,1:T(8,128)(2,1)S(1)} %bitcast.100), channel_id=1, replica_groups=mesh['sx'=4,'sz'=16,'tp'=8] {'tp'}, dimensions={1} | all-to-all | bytes 1048576 | tf_op jit(solution)/shard_map/all_to_all | solution.py:164
  (62 shorter events, 9.7 us)
Async XLA Ops:
  0.0 140.2 %copy-start = (bf16[256,2048]{1,0:T(8,128)(2,1)S(1)}, bf16[256,2048]{1,0:T(8,128)(2,1)}, u32[]{:S(2)}) copy-start(bf16[256,2048]{1,0:T(8,128)(2,1)} %param.19) | copy-start | bytes 3145732
  0.0 60.6 %copy-start.5 = (f32[2048]{0:T(1024)S(1)}, f32[2048]{0:T(1024)}, u32[]{:S(2)}) copy-start(f32[2048]{0:T(1024)} %param.14) | copy-start | bytes 24580
  0.0 60.0 %copy-start.4 = (f32[128]{0:T(128)S(1)}, f32[128]{0:T(128)}, u32[]{:S(2)}) copy-start(f32[128]{0:T(128)} %param.20) | copy-start | bytes 1540
  0.0 60.6 %copy-start.6 = (bf16[2048,2]{0,1:T(2,128)(2,1)S(1)}, bf16[2048,2]{0,1:T(2,128)(2,1)}, u32[]{:S(2)}) copy-start(bf16[2048,2]{0,1:T(2,128)(2,1)} %param.18) | copy-start | bytes 24580
  16.2 62.4 %collective-permute-start = (bf16[128,1,128]{2,0,1:T(8,128)(2,1)}, bf16[128,1,128]{2,0,1:T(8,128)(2,1)}, u32[]{:S(2)}, u32[]{:S(2)}) collective-permute-start(bf16[128,1,128]{2,0,1:T(8,128)(2,1)} %fusion.10), channel_id=1, source_target_pairs={{0,64},{8,72},{16,80},{24,88},{32,96},{40,104},{48,112},{56,120},{... | collective-permute-start | bytes 98312 | tf_op jit(solution)/shard_map/ppermute | solution.py:118
  35.0 65.2 %all-to-all-start = ((bf16[16,2,128,128]{3,2,1,0:T(8,128)(2,1)}), bf16[16,2,128,128]{3,2,1,0:T(8,128)(2,1)S(1)}, u32[]{:S(2)}, u32[]{:S(2)}) async-start(bf16[16,2,128,128]{3,2,1,0:T(8,128)(2,1)} %gather_fusion.1), calls=%async_computation | async-start | bytes 2097152 | tf_op jit(solution)/shard_map/all_to_all | solution.py:90
  45.9 52.8 %collective-permute-start.1 = (bf16[128,1,128]{0,2,1:T(8,128)(2,1)}, bf16[128,1,128]{0,2,1:T(8,128)(2,1)}, u32[]{:S(2)}, u32[]{:S(2)}) collective-permute-start(bf16[128,1,128]{0,2,1:T(8,128)(2,1)} %pad_maximum_fusion.2), channel_id=1, source_target_pairs={{0,64},{8,72},{16,80},{24,88},{32,96},{40,104},{48,112},{56,120},{... | collective-permute-start | bytes 98312 | tf_op jit(solution)/shard_map/ppermute | solution.py:118
  102.5 17.8 %copy-start.2 = (bf16[128,1,128]{0,2,1:T(8,128)(2,1)S(1)}, bf16[128,1,128]{0,2,1:T(8,128)(2,1)}, u32[]{:S(2)}) copy-start(bf16[128,1,128]{0,2,1:T(8,128)(2,1)} %copy.58) | copy-start | bytes 98308
  102.5 17.8 %copy-start.3 = (bf16[128,1,128]{0,2,1:T(8,128)(2,1)S(1)}, bf16[128,1,128]{0,2,1:T(8,128)(2,1)}, u32[]{:S(2)}) copy-start(bf16[128,1,128]{0,2,1:T(8,128)(2,1)} %copy.59) | copy-start | bytes 98308
  116.0 10.2 %all-to-all-start.2 = ((f32[4,128,1,2,2]{1,3,4,2,0:T(2,128)}), f32[4,128,1,2,2]{1,3,4,2,0:T(2,128)S(1)}, u32[]{:S(2)}, u32[]{:S(2)}) async-start(f32[4,128,1,2,2]{1,3,4,2,0:T(2,128)} %copy.66), calls=%async_computation.2 | async-start | bytes 16384 | tf_op jit(solution)/shard_map/all_to_all | solution.py:150
  120.3 34.3 %copy-start.1 = (bf16[128,256]{1,0:T(8,128)(2,1)S(1)}, bf16[128,256]{1,0:T(8,128)(2,1)}, u32[]{:S(2)}) copy-start(bf16[128,256]{1,0:T(8,128)(2,1)} %param.13) | copy-start | bytes 196612
  126.2 13.9 %all-to-all-start.1 = ((f32[4,128,1,2,128]{1,4,3,2,0:T(8,128)}), f32[4,128,1,2,128]{1,4,3,2,0:T(8,128)S(1)}, u32[]{:S(2)}, u32[]{:S(2)}) async-start(f32[4,128,1,2,128]{1,4,3,2,0:T(8,128)} %bitcast.98), calls=%async_computation.1 | async-start | bytes 1048576 | tf_op jit(solution)/shard_map/all_to_all | solution.py:151
where the time goes:
time: 156 us; the launch traced here: 155 us
  starting transfers between devices  41.1 us (26%)
  blocking collectives  40.6 us (26%)
  waiting for transfers between devices  27.6 us (18%)
  matrix products  17.5 us (11%)
  local copies, waits for them, and re-layouts  14 us (9%)
  other arithmetic  13.5 us (9%)
    ppermute x2, starting transfers between devices, per_device(): lax.ppermute((keys_new, values_new), 'sz', partner_pairs)  26 us
    ppermute x2, waiting for transfers between devices, per_device(): lax.ppermute((keys_new, values_new), 'sz', partner_pairs)  18.6 us
    all_gather x1, blocking collectives, per_device(): gathered = lax.all_gather(hidden_in, 'tp', axis=1, tiled=True)  14 us
    all_to_all x1, blocking collectives, per_device(): arrived = lax.all_to_all(pieces, 'tp', 1, 1, tiled=True)  14 us
    all_gather x1, blocking collectives, per_device(): all_queries = lax.all_gather(queries, 'sx', axis=0, tiled=True)  12.6 us
    all_to_all x1, waiting for transfers between devices, per_device(): acc_in = lax.all_to_all(acc, 'sx', 0, 0, tiled=True)  9.05 us
    dot_general x1, matrix products, per_device(): jnp.einsum('tcgd,kcd->tcgk', all_queries, keys_all, preferred_element_typ...  6.72 us
    reduce_sum x1, other arithmetic, per_device(): total = jnp.sum(expo, -1)  6.14 us
  transfers between devices with their start and end apart: 5, of which 2 were waited for; matrix products, arithmetic and copies ran while one was open for 17% of the time, Pallas kernels for 0%

commit v1 on v0

--- a/solution.py
+++ b/solution.py
@@ -8,6 +8,11 @@
 norm_eps = 1e-06
 rope_base = 1000000.0
 masked_score = -1e30
+
+
+def tiled_gather(array, axis, dim):
+    copies = jnp.concatenate([array] * lax.axis_size(axis), axis=dim)
+    return lax.all_to_all(copies, axis, dim, dim, tiled=True)
 
 
 def shifted(value, axis, by):
@@ -92,7 +97,7 @@
     keys_cache = incoming[:, 0].reshape(cache_rows, kv_local, head_dim)
     values_cache = incoming[:, 1].reshape(cache_rows, kv_local, head_dim)
     cache_pos = x_index * cache_rows + jnp.arange(cache_rows, dtype=jnp.int32)
-    gathered = lax.all_gather(hidden_in, "tp", axis=1, tiled=True)
+    gathered = tiled_gather(hidden_in, "tp", 1)
     widened = gathered.astype(jnp.float32)
     normed = (
         widened * lax.rsqrt(jnp.mean(widened * widened, -1, keepdims=True) + norm_eps) * norm_gain

time: 156 us -> 148 us (0.949)
  blocking collectives: 40.6 us -> 27.1 us
  waiting for transfers between devices: 27.6 us -> 33.2 us
  starting transfers between devices: 41.1 us -> 43.3 us
    all_gather x1 -> x0, blocking collectives: 14 us -> none  [per_device(): gathered = lax.all_gather(hidden_in, 'tp', axis=1, tiled=True)]
    ppermute x2, starting transfers between devices: 26 us -> 14.6 us  [per_device(): lax.ppermute((keys_new, values_new), 'sz', partner_pairs)]
    all_to_all x1, starting transfers between devices: 6.04 us -> 15.2 us  [per_device(): incoming = lax.all_to_all(cache_both[peer_groups], 'sz', 0, 0, tiled=True)]
    ppermute x2, waiting for transfers between devices: 18.6 us -> 23.2 us  [per_device(): lax.ppermute((keys_new, values_new), 'sz', partner_pairs)]
    all_to_all x0 -> x1, starting transfers between devices: none -> 4.47 us  [tiled_gather(): return lax.all_to_all(copies, axis, dim, dim, tiled=True)]
    all_to_all x0 -> x1, waiting for transfers between devices: none -> 2.03 us  [tiled_gather(): return lax.all_to_all(copies, axis, dim, dim, tiled=True)]
  transfers between devices with their start and end apart: 5 -> 6, of which waited for: 2 -> 4; matrix products, arithmetic and copies ran while one was open for 17% -> 16% of each run, Pallas kernels for 0% -> 0%
where the time goes in v1:
time: 148 us
  starting transfers between devices  43.3 us (29%)
  waiting for transfers between devices  33.2 us (22%)
  blocking collectives  27.1 us (18%)
  matrix products  16.7 us (11%)
  local copies, waits for them, and re-layouts  13.5 us (9%)
  other arithmetic  12.7 us (9%)
    ppermute x2, waiting for transfers between devices, per_device(): lax.ppermute((keys_new, values_new), 'sz', partner_pairs)  23.2 us
    all_to_all x1, starting transfers between devices, per_device(): incoming = lax.all_to_all(cache_both[peer_groups], 'sz', 0, 0, tiled=True)  15.2 us
    ppermute x2, starting transfers between devices, per_device(): lax.ppermute((keys_new, values_new), 'sz', partner_pairs)  14.6 us
    all_to_all x1, blocking collectives, per_device(): arrived = lax.all_to_all(pieces, 'tp', 1, 1, tiled=True)  14.5 us
    all_gather x1, blocking collectives, per_device(): all_queries = lax.all_gather(queries, 'sx', axis=0, tiled=True)  12.6 us
    all_to_all x1, waiting for transfers between devices, per_device(): acc_in = lax.all_to_all(acc, 'sx', 0, 0, tiled=True)  8.03 us
    dot_general x1, matrix products, per_device(): jnp.einsum('tcgd,kcd->tcgk', all_queries, keys_all, preferred_element_typ...  6.72 us
    reduce_sum x1, other arithmetic, per_device(): total = jnp.sum(expo, -1)  6.14 us
  transfers between devices with their start and end apart: 6, of which 4 were waited for; matrix products, arithmetic and copies ran while one was open for 16% of the time, Pallas kernels for 0%

profile of v1, /device:TPU:32, one launch (start us, length us, event | category | flops | bytes accessed | tf_op | source)
XLA Modules:
  0.0 147.6 jit_solution(15297850145081769609)
XLA Ops:
  0.0 1.0 copy.68
  2.2 4.5 %all-to-all-start.1 = ((bf16[128,8,256]{2,0,1:T(8,128)(2,1)}), bf16[128,8,256]{2,0,1:T(8,128)(2,1)S(1)}, u32[]{:S(2)}, u32[]{:S(2)}) async-start(bf16[128,8,256]{2,0,1:T(8,128)(2,1)} %copy.76), calls=%async_computation.1 | async-start | bytes 1048576 | tf_op jit(solution)/shard_map/all_to_all | solution.py:15
  6.8 1.3 gather_fusion
  8.2 1.2 dynamic_slice.3
  11.1 1.7 %gather_fusion.1 = bf16[16,2,128,128]{3,2,1,0:T(8,128)(2,1)} fusion(bf16[2,2,128,128]{3,2,0,1:T(8,128)(2,1)S(1)} %pad_maximum_fusion, s32[1024]{0:T(1024)S(1)} %pad_clamp_fusion), kind=kCustom, calls=%fused_computation.1 | custom fusion | bytes 2097216 | tf_op jit(solution)/shard_map/gather | solution.py:95
  12.8 2.2 %pad_add_fusion = pred[512,2304]{0,1:T(8,128)(4,1)S(1)} fusion(pred[512,256]{0,1:T(8,128)(4,1)S(1)} %broadcast_compare_fusion, pred[2304]{0:T(1024)(128)(4,1)S(1)} %pad.9.clone), kind=kLoop, calls=%fused_computation.9 | loop fusion | flops 1179648 | bytes 1313024 | tf_op jit(solution)/shard_map/concatenate | solution.py:135
  15.0 2.0 %all-to-all-done.1 = bf16[128,8,256]{2,0,1:T(8,128)(2,1)S(1)} async-done(((bf16[128,8,256]{2,0,1:T(8,128)(2,1)}), bf16[128,8,256]{2,0,1:T(8,128)(2,1)S(1)}, u32[]{:S(2)}, u32[]{:S(2)}) %all-to-all-start.1) | async-done | bytes 524320 | tf_op jit(solution)/shard_map/all_to_all | solution.py:15
  17.0 15.2 %all-to-all-start = ((bf16[16,2,128,128]{3,2,1,0:T(8,128)(2,1)}), bf16[16,2,128,128]{3,2,1,0:T(8,128)(2,1)}, u32[]{:S(2)}, u32[]{:S(2)}) async-start(bf16[16,2,128,128]{3,2,1,0:T(8,128)(2,1)} %gather_fusion.1), calls=%async_computation | async-start | bytes 2097152 | tf_op jit(solution)/shard_map/all_to_all | solution.py:95
  34.2 1.4 fusion.10
  35.6 11.2 %collective-permute-start = (bf16[128,1,128]{2,0,1:T(8,128)(2,1)S(1)}, bf16[128,1,128]{2,0,1:T(8,128)(2,1)S(1)}, u32[]{:S(2)}, u32[]{:S(2)}) collective-permute-start(bf16[128,1,128]{2,0,1:T(8,128)(2,1)S(1)} %fusion.10), channel_id=1, source_target_pairs={{0,64},{8,72},{16,80},{24,88},{32,96},{40,104},{48,112},{56,120},{... | collective-permute-start | bytes 98312 | tf_op jit(solution)/shard_map/ppermute | solution.py:123
  46.8 1.6 %fusion.48 = f32[128,256]{1,0:T(8,128)S(1)} fusion(bf16[128,2048]{0,1:T(8,128)(2,1)S(1)} %fusion.15, bf16[2048,256]{1,0:T(8,128)(2,1)} %param.15), kind=kOutput, calls=%fused_computation.106 | convolution fusion | flops 134217728 | bytes 1703936 | tf_op jit(solution)/shard_map/dot_general | solution.py:106
  48.4 1.4 multiply_reduce_fusion.3
  50.1 3.4 %collective-permute-start.1 = (bf16[128,1,128]{0,2,1:T(8,128)(2,1)S(1)}, bf16[128,1,128]{0,2,1:T(8,128)(2,1)S(1)}, u32[]{:S(2)}, u32[]{:S(2)}) collective-permute-start(bf16[128,1,128]{0,2,1:T(8,128)(2,1)S(1)} %pad_maximum_fusion.2), channel_id=1, source_target_pairs={{0,64},{8,72},{16,80},{24,88},{32,96},{40,104},{48,112},{56,120},{... | collective-permute-start | bytes 98312 | tf_op jit(solution)/shard_map/ppermute | solution.py:123
  54.3 12.6 %all_gather.3 = bf16[512,1,2,128]{3,0,2,1:T(8,128)(2,1)S(1)} all-gather(bf16[128,1,2,128]{3,0,2,1:T(8,128)(2,1)S(1)} %pad_maximum_fusion.1), channel_id=1, replica_groups=mesh['sx'=4,'sz'=16,'tp'=8] {'sx'}, dimensions={0}, use_global_device_ids=true | all-gather | bytes 327680 | tf_op jit(solution)/shard_map/all_gather | solution.py:125
  68.4 21.5 %collective-permute-done = bf16[128,1,128]{2,0,1:T(8,128)(2,1)S(1)} collective-permute-done((bf16[128,1,128]{2,0,1:T(8,128)(2,1)S(1)}, bf16[128,1,128]{2,0,1:T(8,128)(2,1)S(1)}, u32[]{:S(2)}, u32[]{:S(2)}) %collective-permute-start) | collective-permute-done | bytes 32800 | tf_op jit(solution)/shard_map/ppermute | solution.py:123
  90.6 1.7 %collective-permute-done.1 = bf16[128,1,128]{0,2,1:T(8,128)(2,1)S(1)} collective-permute-done((bf16[128,1,128]{0,2,1:T(8,128)(2,1)S(1)}, bf16[128,1,128]{0,2,1:T(8,128)(2,1)S(1)}, u32[]{:S(2)}, u32[]{:S(2)}) %collective-permute-start.1) | collective-permute-done | bytes 32800 | tf_op jit(solution)/shard_map/ppermute | solution.py:123
  93.0 2.1 %fusion.47 = (bf16[16,1,128,128]{3,2,1,0:T(8,128)(2,1)S(1)}, bf16[16,1,128,128]{3,2,1,0:T(8,128)(2,1)}) fusion(bf16[16,2,128,128]{3,2,1,0:T(8,128)(2,1)} %all-to-all-done), kind=kLoop, calls=%fused_computation.105 | loop fusion | bytes 2097152 | tf_op jit(solution)/shard_map/slice | solution.py:98
  95.3 6.7 %fusion = (f32[512,2]{0,1:T(2,128)S(1)}, f32[2304,512,2]{1,0,2:T(8,128)}) fusion(pred[512,2304]{0,1:T(8,128)(4,1)S(1)} %pad_add_fusion, bf16[512,1,2,128]{3,0,2,1:T(8,128)(2,1)S(1)} %all_gather.3, bf16[128,1,128]{2,0,1:T(8,128)(2,1)} %copy.81, bf16[128,1,128]{2,0,1:T(8,128)(2,1)} %copy.80, bf16[2048,1,128]{2,0,1:T(8,128)(2,1)} %bitcast.114), kind=kOutput, calls=%fused_computation.4 | convolution fusion | flops 612826112 | bytes 11472896 | tf_op jit(solution)/shard_map/tcgd,kcd->tcgk/dot_general | solution.py:142
  102.0 6.1 %fusion.1 = f32[512,2]{0,1:T(2,128)S(1)} fusion(f32[2304,512,2]{1,0,2:T(8,128)} %get-tuple-element.16, f32[512,2]{0,1:T(2,128)S(1)} %get-tuple-element.15, pred[512,2304]{0,1:T(8,128)(4,1)S(1)} %pad_add_fusion), kind=kLoop, calls=%fused_computation.5 | loop fusion | flops 11795456 | bytes 10625024 | tf_op jit(solution)/shard_map/reduce_sum | solution.py:149
  108.8 4.3 %all-to-all-start.3 = ((f32[4,128,1,2,2]{1,3,4,2,0:T(2,128)}), f32[4,128,1,2,2]{1,3,4,2,0:T(2,128)S(1)}, u32[]{:S(2)}, u32[]{:S(2)}) async-start(f32[4,128,1,2,2]{1,3,4,2,0:T(2,128)} %copy.86), calls=%async_computation.3 | async-start | bytes 16384 | tf_op jit(solution)/shard_map/all_to_all | solution.py:155
  113.1 5.1 %fusion.7 = f32[1,2,16,4,8,128]{5,4,3,2,1,0:T(8,128)S(1)} fusion(f32[2304,512,2]{1,0,2:T(8,128)} %get-tuple-element.16, f32[512,2]{0,1:T(2,128)S(1)} %get-tuple-element.15, pred[512,2304]{0,1:T(8,128)(4,1)S(1)} %pad_add_fusion, bf16[128,1,128]{0,2,1:T(8,128)(2,1)S(1)} %copy-done.3, bf16[128,1,128]{0,2,1:T(8,128)(2,1)S(1)} %copy-done.2, ...), kind=kOutput, calls=%fused_computation.12 | convolution fusion | flops 617545728 | bytes 11735040 | tf_op jit(solution)/shard_map/tcgk,kcd->tcgd/dot_general | solution.py:150
  119.0 4.8 %all-to-all-start.2 = ((f32[4,128,1,2,128]{1,4,3,2,0:T(8,128)}), f32[4,128,1,2,128]{1,4,3,2,0:T(8,128)S(1)}, u32[]{:S(2)}, u32[]{:S(2)}) async-start(f32[4,128,1,2,128]{1,4,3,2,0:T(8,128)} %bitcast.109), calls=%async_computation.2 | async-start | bytes 1048576 | tf_op jit(solution)/shard_map/all_to_all | solution.py:156
  123.9 8.0 %all-to-all-done.2 = f32[4,128,1,2,128]{1,4,3,2,0:T(8,128)S(1)} async-done(((f32[4,128,1,2,128]{1,4,3,2,0:T(8,128)}), f32[4,128,1,2,128]{1,4,3,2,0:T(8,128)S(1)}, u32[]{:S(2)}, u32[]{:S(2)}) %all-to-all-start.2) | async-done | bytes 524320 | tf_op jit(solution)/shard_map/all_to_all | solution.py:156
  132.4 14.5 %all_to_all.29 = bf16[128,8,256]{2,0,1:T(8,128)(2,1)S(1)} all-to-all(bf16[128,8,256]{2,0,1:T(8,128)(2,1)S(1)} %bitcast.111), channel_id=1, replica_groups=mesh['sx'=4,'sz'=16,'tp'=8] {'tp'}, dimensions={1} | all-to-all | bytes 1048576 | tf_op jit(solution)/shard_map/all_to_all | solution.py:169
  (77 shorter events, 11.0 us)
Async XLA Ops:
  0.0 132.0 %copy-start = (bf16[256,2048]{1,0:T(8,128)(2,1)S(1)}, bf16[256,2048]{1,0:T(8,128)(2,1)}, u32[]{:S(2)}) copy-start(bf16[256,2048]{1,0:T(8,128)(2,1)} %param.19) | copy-start | bytes 3145732
  0.0 33.8 %copy-start.4 = (f32[2048]{0:T(1024)S(1)}, f32[2048]{0:T(1024)}, u32[]{:S(2)}) copy-start(f32[2048]{0:T(1024)} %param.14) | copy-start | bytes 24580
  0.0 49.8 %copy-start.6 = (f32[128]{0:T(128)S(1)}, f32[128]{0:T(128)}, u32[]{:S(2)}) copy-start(f32[128]{0:T(128)} %param.21) | copy-start | bytes 1540
  0.0 53.8 %copy-start.7 = (f32[128]{0:T(128)S(1)}, f32[128]{0:T(128)}, u32[]{:S(2)}) copy-start(f32[128]{0:T(128)} %param.20) | copy-start | bytes 1540
  0.0 54.1 %copy-start.5 = (bf16[2048,2]{0,1:T(2,128)(2,1)S(1)}, bf16[2048,2]{0,1:T(2,128)(2,1)}, u32[]{:S(2)}) copy-start(bf16[2048,2]{0,1:T(2,128)(2,1)} %param.18) | copy-start | bytes 24580
  2.2 14.8 %all-to-all-start.1 = ((bf16[128,8,256]{2,0,1:T(8,128)(2,1)}), bf16[128,8,256]{2,0,1:T(8,128)(2,1)S(1)}, u32[]{:S(2)}, u32[]{:S(2)}) async-start(bf16[128,8,256]{2,0,1:T(8,128)(2,1)} %copy.76), calls=%async_computation.1 | async-start | bytes 1048576 | tf_op jit(solution)/shard_map/all_to_all | solution.py:15
  17.0 75.9 %all-to-all-start = ((bf16[16,2,128,128]{3,2,1,0:T(8,128)(2,1)}), bf16[16,2,128,128]{3,2,1,0:T(8,128)(2,1)}, u32[]{:S(2)}, u32[]{:S(2)}) async-start(bf16[16,2,128,128]{3,2,1,0:T(8,128)(2,1)} %gather_fusion.1), calls=%async_computation | async-start | bytes 2097152 | tf_op jit(solution)/shard_map/all_to_all | solution.py:95
  35.6 54.3 %collective-permute-start = (bf16[128,1,128]{2,0,1:T(8,128)(2,1)S(1)}, bf16[128,1,128]{2,0,1:T(8,128)(2,1)S(1)}, u32[]{:S(2)}, u32[]{:S(2)}) collective-permute-start(bf16[128,1,128]{2,0,1:T(8,128)(2,1)S(1)} %fusion.10), channel_id=1, source_target_pairs={{0,64},{8,72},{16,80},{24,88},{32,96},{40,104},{48,112},{56,120},{... | collective-permute-start | bytes 98312 | tf_op jit(solution)/shard_map/ppermute | solution.py:123
  50.1 42.1 %collective-permute-start.1 = (bf16[128,1,128]{0,2,1:T(8,128)(2,1)S(1)}, bf16[128,1,128]{0,2,1:T(8,128)(2,1)S(1)}, u32[]{:S(2)}, u32[]{:S(2)}) collective-permute-start(bf16[128,1,128]{0,2,1:T(8,128)(2,1)S(1)} %pad_maximum_fusion.2), channel_id=1, source_target_pairs={{0,64},{8,72},{16,80},{24,88},{32,96},{40,104},{48,112},{56,120},{... | collective-permute-start | bytes 98312 | tf_op jit(solution)/shard_map/ppermute | solution.py:123
  95.3 17.8 %copy-start.2 = (bf16[128,1,128]{0,2,1:T(8,128)(2,1)S(1)}, bf16[128,1,128]{0,2,1:T(8,128)(2,1)}, u32[]{:S(2)}) copy-start(bf16[128,1,128]{0,2,1:T(8,128)(2,1)} %copy.78) | copy-start | bytes 98308
  95.3 17.8 %copy-start.3 = (bf16[128,1,128]{0,2,1:T(8,128)(2,1)S(1)}, bf16[128,1,128]{0,2,1:T(8,128)(2,1)}, u32[]{:S(2)}) copy-start(bf16[128,1,128]{0,2,1:T(8,128)(2,1)} %copy.79) | copy-start | bytes 98308
  108.8 10.2 %all-to-all-start.3 = ((f32[4,128,1,2,2]{1,3,4,2,0:T(2,128)}), f32[4,128,1,2,2]{1,3,4,2,0:T(2,128)S(1)}, u32[]{:S(2)}, u32[]{:S(2)}) async-start(f32[4,128,1,2,2]{1,3,4,2,0:T(2,128)} %copy.86), calls=%async_computation.3 | async-start | bytes 16384 | tf_op jit(solution)/shard_map/all_to_all | solution.py:155
  113.1 33.8 %copy-start.1 = (bf16[128,256]{1,0:T(8,128)(2,1)S(1)}, bf16[128,256]{1,0:T(8,128)(2,1)}, u32[]{:S(2)}) copy-start(bf16[128,256]{1,0:T(8,128)(2,1)} %param.13) | copy-start | bytes 196612
  119.0 12.9 %all-to-all-start.2 = ((f32[4,128,1,2,128]{1,4,3,2,0:T(8,128)}), f32[4,128,1,2,128]{1,4,3,2,0:T(8,128)S(1)}, u32[]{:S(2)}, u32[]{:S(2)}) async-start(f32[4,128,1,2,128]{1,4,3,2,0:T(8,128)} %bitcast.109), calls=%async_computation.2 | async-start | bytes 1048576 | tf_op jit(solution)/shard_map/all_to_all | solution.py:156
